TPU v7x, 256 devices: a whole 4x4x8 slice. The times are simulated.
256 devices in a mesh: dp: 32 (over z, y), expert: 8 (over x, core).
Axes of the slice: x: 4, y: 4, z: 8, core: 2. Of those that a mesh axis runs over, the one named last changes fastest.
Arguments:
- tokens: bfloat16 [32768, 2048], P(('dp', 'expert')), may hold values from -6 to 6
- routes: int32 [32768, 2], P(('dp', 'expert')), may hold values from 0 to 127, all different within a row; in each aligned block of 128 rows (0 to 127, 128 to 255, ...) at most 4 rows name the same one
- gate_codes: int32 [32768, 2], P(('dp', 'expert')), may hold values from 1 to 1024
- w_gate: bfloat16 [256, 2048, 384], P(('dp', 'expert')), may hold values from -0.125 to 0.125
- w_up: bfloat16 [256, 2048, 384], P(('dp', 'expert')), may hold values from -0.125 to 0.125
- w_down: bfloat16 [256, 384, 2048], P(('dp', 'expert')), may hold values from -0.21875 to 0.21875
- cot: bfloat16 [32768, 2048], P(('dp', 'expert')), may hold values from -6 to 6
Outputs:
- mixed: bfloat16 [32768, 2048], P(('dp', 'expert'))
- d_tokens: bfloat16 [32768, 2048], P(('dp', 'expert'))
- d_gate: bfloat16 [256, 2048, 384], P(('dp', 'expert'))
- d_up: bfloat16 [256, 2048, 384], P(('dp', 'expert'))
- d_down: bfloat16 [256, 384, 2048], P(('dp', 'expert'))
Inputs may be any that keep to these rules, and one draw needn't show every extreme that they name: `routes`: each row names 2 different experts; among the 128 rows of one device no expert is named more than 4 times, a bound that some block reaches. `gate_codes`: the gate weight is the value divided by 1024.
All inputs are finite; a program needn't handle non-finite values.
Results may differ from a plain program's by a relative error of at most 0.012.
Values may be sent and summed in bfloat16 or wider, within the bound.
No kernel may reach another device: no remote copies, remote signals or barrier semaphores. Data moves between devices by JAX's collectives and lax.ppermute only.
A program may use at most 128 MiB of HBM per device.

v0:
```python
import jax
import jax.numpy as jnp
from jax import lax
from jax.sharding import PartitionSpec as P


def expert_work(xrows, qrows, w_gate, w_up, w_down):
    act = jnp.dot(xrows, w_gate, preferred_element_type=jnp.float32)
    upv = jnp.dot(xrows, w_up, preferred_element_type=jnp.float32)
    sig = jax.nn.sigmoid(act)
    silu = act * sig
    hidden = (silu * upv).astype(jnp.bfloat16)
    outv = jnp.dot(hidden, w_down, preferred_element_type=jnp.float32).astype(jnp.bfloat16)
    dhid = jnp.dot(qrows, w_down.T, preferred_element_type=jnp.float32)
    dact = (dhid * upv * sig * (1.0 + act * (1.0 - sig))).astype(jnp.bfloat16)
    dupv = (dhid * silu).astype(jnp.bfloat16)
    pgrad = (
        jnp.dot(dact, w_gate.T, preferred_element_type=jnp.float32)
        + jnp.dot(dupv, w_up.T, preferred_element_type=jnp.float32)
    ).astype(jnp.bfloat16)
    grad_g = jnp.dot(xrows.T, dact, preferred_element_type=jnp.float32).astype(jnp.bfloat16)
    grad_u = jnp.dot(xrows.T, dupv, preferred_element_type=jnp.float32).astype(jnp.bfloat16)
    grad_d = jnp.dot(hidden.T, qrows, preferred_element_type=jnp.float32).astype(jnp.bfloat16)
    return (outv, pgrad, grad_g, grad_u, grad_d)


def reorder(index, n_data, n_group, slots):
    device = index // slots
    within = index % slots
    return (device % n_group * n_data + device // n_group) * slots + within


def group_major(row_pair, n_data, n_group, slots):
    return row_pair.reshape(n_data, n_group, slots).transpose(1, 0, 2).reshape(-1)


def local(tokens, routes, gate_codes, w_gate, w_up, w_down, cot):
    tok_rows, top = routes.shape
    width = tokens.shape[1]
    n_data = lax.axis_size("dp")
    n_group = lax.axis_size("expert")
    devices = n_data * n_group
    experts = devices // 2
    most = max(2, 2 * tok_rows * top // experts)
    pairs = tok_rows * top
    expert_ids = routes.reshape(pairs)
    onehot = (expert_ids[:, None] == jnp.arange(experts, dtype=jnp.int32)[None, :]).astype(
        jnp.int32
    )
    before = jnp.cumsum(onehot, axis=0) - onehot
    position = jnp.sum(before * onehot, axis=1)
    gates = gate_codes.reshape(pairs).astype(jnp.float32) / 1024.0
    qpairs = (
        (gates.reshape(tok_rows, top, 1) * cot.astype(jnp.float32)[:, None, :])
        .astype(jnp.bfloat16)
        .reshape(pairs, width)
    )
    tok_pad = jnp.concatenate([tokens, jnp.zeros((1, width), jnp.bfloat16)], axis=0)
    q_pad = jnp.concatenate([qpairs, jnp.zeros((1, width), jnp.bfloat16)], axis=0)
    pair_ids = jnp.arange(pairs, dtype=jnp.int32)
    wg = w_gate[0]
    wu = w_up[0]
    wd = w_down[0]
    total = devices * most
    halves = jnp.arange(2, dtype=jnp.int32)
    targets = (2 * expert_ids[:, None] + halves[None, :]) * most + position[:, None]
    row_pair = (
        jnp.full((total,), pairs, jnp.int32).at[targets.reshape(-1)].set(jnp.repeat(pair_ids, 2))
    )
    row_pair = group_major(row_pair, n_data, n_group, most)
    row_token = jnp.where(row_pair < pairs, row_pair // top, tok_rows)
    xsend = tok_pad[row_token].reshape(n_group, n_data, most * width)
    qsend = q_pad[row_pair].reshape(n_group, n_data, most * width)
    xrecv, qrecv = (
        lax.all_to_all(
            lax.all_to_all(xsend, "dp", split_axis=1, concat_axis=1, tiled=True),
            "expert",
            split_axis=0,
            concat_axis=0,
            tiled=True,
        ),
        lax.all_to_all(
            lax.all_to_all(qsend, "dp", split_axis=1, concat_axis=1, tiled=True),
            "expert",
            split_axis=0,
            concat_axis=0,
            tiled=True,
        ),
    )
    outv, pgrad, grad_g, grad_u, grad_d = expert_work(
        xrecv.reshape(total, width), qrecv.reshape(total, width), wg, wu, wd
    )
    oback, pback = (
        lax.all_to_all(
            lax.all_to_all(
                outv.reshape(n_group, n_data, most * width),
                "dp",
                split_axis=1,
                concat_axis=1,
                tiled=True,
            ),
            "expert",
            split_axis=0,
            concat_axis=0,
            tiled=True,
        ),
        lax.all_to_all(
            lax.all_to_all(
                pgrad.reshape(n_group, n_data, most * width),
                "dp",
                split_axis=1,
                concat_axis=1,
                tiled=True,
            ),
            "expert",
            split_axis=0,
            concat_axis=0,
            tiled=True,
        ),
    )
    back_idx = reorder(targets, n_data, n_group, most)
    pair_out = jnp.sum(oback.reshape(total, width)[back_idx].astype(jnp.float32), axis=1)
    pair_grad = jnp.sum(pback.reshape(total, width)[back_idx].astype(jnp.float32), axis=1)
    mixed = jnp.sum((gates[:, None] * pair_out).reshape(tok_rows, top, width), axis=1).astype(
        jnp.bfloat16
    )
    d_tokens = jnp.sum(pair_grad.reshape(tok_rows, top, width), axis=1).astype(jnp.bfloat16)
    return (mixed, d_tokens, grad_g[None], grad_u[None], grad_d[None])


def solution(mesh):
    placed = (
        P(("dp", "expert"), None),
        P(("dp", "expert"), None),
        P(("dp", "expert"), None),
        P(("dp", "expert"), None, None),
        P(("dp", "expert"), None, None),
        P(("dp", "expert"), None, None),
        P(("dp", "expert"), None),
    )
    return jax.shard_map(
        local,
        mesh=mesh,
        in_specs=placed,
        out_specs=(
            P(("dp", "expert"), None),
            P(("dp", "expert"), None),
            P(("dp", "expert"), None, None),
            P(("dp", "expert"), None, None),
            P(("dp", "expert"), None, None),
        ),
        check_vma=False,
    )
```

profile of v0, /device:TPU:11, one launch (start us, length us, event | category | flops | bytes accessed | tf_op | source)
XLA Modules:
  0.0 744.6 jit_solution(10845163730356967747)
XLA Ops:
  0.7 0.9 copy.78
  1.7 0.1 eq.29
  2.0 0.2 fusion.18
  2.3 0.2 fusion.20
  2.5 0.1 multiply_add_fusion.1
  2.6 0.1 add.201
  2.9 2.4 scatter_custom_fusion
  5.8 6.1 gather_fusion
  11.9 7.9 %reshape.463 = bf16[8,32,8192]{2,1,0:T(8,128)(2,1)} reshape(bf16[1024,2048]{1,0:T(8,128)(2,1)} %gather_fusion) | data formatting | bytes 8388608 | tf_op jit(solution)/shard_map/reshape | solution.py:72
  19.8 6.5 copy.83
  26.2 11.3 %all-to-all-start = ((bf16[8,32,8192]{2,0,1:T(8,128)(2,1)}), bf16[8,32,8192]{2,0,1:T(8,128)(2,1)}, u32[]{:S(2)}, u32[]{:S(2)}) async-start(bf16[8,32,8192]{2,0,1:T(8,128)(2,1)} %copy.83), calls=%async_computation | async-start | bytes 8388608 | tf_op jit(solution)/shard_map/all_to_all | solution.py:76
  37.9 2.4 mul.120
  40.3 3.7 mul.121
  44.0 1.8 multiply_convert_fusion
  45.9 6.0 gather_fusion.2
  51.9 7.9 %reshape.467 = bf16[8,32,8192]{2,1,0:T(8,128)(2,1)} reshape(bf16[1024,2048]{1,0:T(8,128)(2,1)} %gather_fusion.2) | data formatting | bytes 8388608 | tf_op jit(solution)/shard_map/reshape | solution.py:73
  59.8 6.4 copy.89
  66.2 65.7 %all-to-all-done = bf16[8,32,8192]{2,0,1:T(8,128)(2,1)} async-done(((bf16[8,32,8192]{2,0,1:T(8,128)(2,1)}), bf16[8,32,8192]{2,0,1:T(8,128)(2,1)}, u32[]{:S(2)}, u32[]{:S(2)}) %all-to-all-start) | async-done | bytes 4194336 | tf_op jit(solution)/shard_map/all_to_all | solution.py:76
  132.0 18.5 %all-to-all-start.4 = ((bf16[8,32,8192]{2,0,1:T(8,128)(2,1)}), bf16[8,32,8192]{2,0,1:T(8,128)(2,1)}, u32[]{:S(2)}, u32[]{:S(2)}) async-start(bf16[8,32,8192]{2,0,1:T(8,128)(2,1)} %copy.89), calls=%async_computation.4 | async-start | bytes 8388608 | tf_op jit(solution)/shard_map/all_to_all | solution.py:83
  150.5 6.4 copy.84
  156.9 88.0 %all-to-all-done.4 = bf16[8,32,8192]{2,0,1:T(8,128)(2,1)} async-done(((bf16[8,32,8192]{2,0,1:T(8,128)(2,1)}), bf16[8,32,8192]{2,0,1:T(8,128)(2,1)}, u32[]{:S(2)}, u32[]{:S(2)}) %all-to-all-start.4) | async-done | bytes 4194336 | tf_op jit(solution)/shard_map/all_to_all | solution.py:83
  244.9 7.8 %all-to-all-start.1 = ((bf16[8,32,8192]{2,1,0:T(8,128)(2,1)}), bf16[8,32,8192]{2,1,0:T(8,128)(2,1)}, u32[]{:S(2)}, u32[]{:S(2)}) async-start(bf16[8,32,8192]{2,1,0:T(8,128)(2,1)} %copy.84), calls=%async_computation.1 | async-start | bytes 8388608 | tf_op jit(solution)/shard_map/all_to_all | solution.py:75
  252.7 6.4 copy.90
  259.1 41.4 %all-to-all-done.1 = bf16[8,32,8192]{2,1,0:T(8,128)(2,1)} async-done(((bf16[8,32,8192]{2,1,0:T(8,128)(2,1)}), bf16[8,32,8192]{2,1,0:T(8,128)(2,1)}, u32[]{:S(2)}, u32[]{:S(2)}) %all-to-all-start.1) | async-done | bytes 4194336 | tf_op jit(solution)/shard_map/all_to_all | solution.py:75
  300.6 6.4 all-to-all-start.5
  307.0 7.9 %reshape.464 = bf16[1024,2048]{1,0:T(8,128)(2,1)} reshape(bf16[8,32,8192]{2,1,0:T(8,128)(2,1)} %all-to-all-done.1) | data formatting | bytes 8388608 | tf_op jit(solution)/shard_map/reshape | solution.py:91
  314.9 6.3 fusion.7
  321.2 3.5 fusion.11
  324.7 30.2 %all-to-all-done.5 = bf16[8,32,8192]{2,1,0:T(8,128)(2,1)} async-done(((bf16[8,32,8192]{2,1,0:T(8,128)(2,1)}), bf16[8,32,8192]{2,1,0:T(8,128)(2,1)}, u32[]{:S(2)}, u32[]{:S(2)}) %all-to-all-start.5) | async-done | bytes 4194336 | tf_op jit(solution)/shard_map/all_to_all | solution.py:82
  354.8 8.0 %reshape.468 = bf16[1024,2048]{1,0:T(8,128)(2,1)} reshape(bf16[8,32,8192]{2,1,0:T(8,128)(2,1)} %all-to-all-done.5) | data formatting | bytes 8388608 | tf_op jit(solution)/shard_map/reshape | solution.py:91
  362.8 7.1 multiply_convert_fusion.1
  369.9 0.9 copy-done.12
  370.8 4.3 convolution_convert_fusion
  375.1 7.9 %reshape.465 = bf16[8,32,8192]{2,1,0:T(8,128)(2,1)} reshape(bf16[1024,2048]{1,0:T(8,128)(2,1)} %convolution_convert_fusion) | data formatting | bytes 8388608 | tf_op jit(solution)/shard_map/reshape | solution.py:96
  383.0 6.4 copy.85
  389.4 5.1 all-to-all-start.2
  394.5 3.6 fusion.9
  398.2 4.3 add_convert_fusion
  402.5 7.9 %reshape.469 = bf16[8,32,8192]{2,1,0:T(8,128)(2,1)} reshape(bf16[1024,2048]{1,0:T(8,128)(2,1)} %add_convert_fusion) | data formatting | bytes 8388608 | tf_op jit(solution)/shard_map/reshape | solution.py:109
  410.5 6.4 copy.91
  416.9 71.7 %all-to-all-done.2 = bf16[8,32,8192]{2,0,1:T(8,128)(2,1)} async-done(((bf16[8,32,8192]{2,0,1:T(8,128)(2,1)}), bf16[8,32,8192]{2,0,1:T(8,128)(2,1)}, u32[]{:S(2)}, u32[]{:S(2)}) %all-to-all-start.2) | async-done | bytes 4194336 | tf_op jit(solution)/shard_map/all_to_all | solution.py:95
  488.6 6.9 all-to-all-start.6
  495.5 6.5 copy.86
  502.0 90.9 %all-to-all-done.6 = bf16[8,32,8192]{2,0,1:T(8,128)(2,1)} async-done(((bf16[8,32,8192]{2,0,1:T(8,128)(2,1)}), bf16[8,32,8192]{2,0,1:T(8,128)(2,1)}, u32[]{:S(2)}, u32[]{:S(2)}) %all-to-all-start.6) | async-done | bytes 4194336 | tf_op jit(solution)/shard_map/all_to_all | solution.py:108
  592.9 6.0 all-to-all-start.3
  598.9 6.5 copy.92
  605.4 41.4 %all-to-all-done.3 = bf16[8,32,8192]{2,1,0:T(8,128)(2,1)} async-done(((bf16[8,32,8192]{2,1,0:T(8,128)(2,1)}), bf16[8,32,8192]{2,1,0:T(8,128)(2,1)}, u32[]{:S(2)}, u32[]{:S(2)}) %all-to-all-start.3) | async-done | bytes 4194336 | tf_op jit(solution)/shard_map/all_to_all | solution.py:94
  646.8 6.6 all-to-all-start.7
  653.3 0.3 compare_select_fusion
  653.9 5.3 fusion.2
  659.2 3.6 fusion.1
  662.8 3.6 fusion
  666.4 7.9 %reshape.466 = bf16[1024,2048]{1,0:T(8,128)(2,1)} reshape(bf16[8,32,8192]{2,1,0:T(8,128)(2,1)} %all-to-all-done.3) | data formatting | bytes 8388608 | tf_op jit(solution)/shard_map/reshape | solution.py:122
  674.3 8.0 %gather_fusion.1 = bf16[512,2048]{1,0:T(8,128)(2,1)} fusion(bf16[1024,2048]{1,0:T(8,128)(2,1)} %reshape.466, s32[1024]{0:T(1024)S(1)} %pad_clamp_fusion), kind=kCustom, calls=%fused_computation.1 | custom fusion | bytes 4196352 | tf_op jit(solution)/shard_map/gather | solution.py:122
  682.2 5.6 reshape.514
  687.9 8.5 %reduce_sum.48 = f32[256,2048]{1,0:T(8,128)} reduce(f32[256,2,2048]{2,1,0:T(2,128)} %reshape.514, f32[]{:T(128)} %constant.88.clone.1), dimensions={1}, to_apply=%region_4.5 | reduce | flops 524288 | bytes 6291460 | tf_op jit(solution)/shard_map/reduce_sum | solution.py:122
  696.4 3.5 reduce_sum.49
  699.9 5.6 multiply_reduce_fusion
  705.5 7.9 %reshape.470 = bf16[1024,2048]{1,0:T(8,128)(2,1)} reshape(bf16[8,32,8192]{2,1,0:T(8,128)(2,1)} %all-to-all-done.7) | data formatting | bytes 8388608 | tf_op jit(solution)/shard_map/reshape | solution.py:123
  713.4 8.2 %gather_fusion.3 = bf16[512,2048]{1,0:T(8,128)(2,1)} fusion(bf16[1024,2048]{1,0:T(8,128)(2,1)} %reshape.470, s32[1024]{0:T(1024)S(1)} %pad_clamp_fusion), kind=kCustom, calls=%fused_computation.3 | custom fusion | bytes 4196352 | tf_op jit(solution)/shard_map/gather | solution.py:123
  721.6 5.5 reshape.515
  727.1 8.5 %reduce_sum.51 = f32[256,2048]{1,0:T(8,128)} reduce(f32[256,2,2048]{2,1,0:T(2,128)} %reshape.515, f32[]{:T(128)} %constant.88.clone.1), dimensions={1}, to_apply=%region_6.7 | reduce | flops 524288 | bytes 6291460 | tf_op jit(solution)/shard_map/reduce_sum | solution.py:123
  735.6 3.6 reshape.471
  739.2 5.0 reduce_sum.52
  (53 shorter events, 1.4 us)
Async XLA Ops:
  0.6 362.2 %copy-start = (bf16[1,384,2048]{2,1,0:T(8,128)(2,1)S(1)}, bf16[1,384,2048]{2,1,0:T(8,128)(2,1)}, u32[]{:S(2)}) copy-start(bf16[1,384,2048]{2,1,0:T(8,128)(2,1)} %param.12) | copy-start | bytes 4718596
  0.6 5.1 copy-start.10
  26.2 11.3 %copy-start.11 = (s32[128,2]{0,1:T(2,128)S(1)}, s32[128,2]{0,1:T(2,128)}, u32[]{:S(2)}) copy-start(s32[128,2]{0,1:T(2,128)} %param.9) | copy-start | bytes 3076
  26.2 11.6 %copy-start.9 = (bf16[128,2048]{1,0:T(8,128)(2,1)S(1)}, bf16[128,2048]{1,0:T(8,128)(2,1)}, u32[]{:S(2)}) copy-start(bf16[128,2048]{1,0:T(8,128)(2,1)} %param.13) | copy-start | bytes 1572868
  26.2 105.7 %all-to-all-start = ((bf16[8,32,8192]{2,0,1:T(8,128)(2,1)}), bf16[8,32,8192]{2,0,1:T(8,128)(2,1)}, u32[]{:S(2)}, u32[]{:S(2)}) async-start(bf16[8,32,8192]{2,0,1:T(8,128)(2,1)} %copy.83), calls=%async_computation | async-start | bytes 8388608 | tf_op jit(solution)/shard_map/all_to_all | solution.py:76
  132.0 112.9 %all-to-all-start.4 = ((bf16[8,32,8192]{2,0,1:T(8,128)(2,1)}), bf16[8,32,8192]{2,0,1:T(8,128)(2,1)}, u32[]{:S(2)}, u32[]{:S(2)}) async-start(bf16[8,32,8192]{2,0,1:T(8,128)(2,1)} %copy.89), calls=%async_computation.4 | async-start | bytes 8388608 | tf_op jit(solution)/shard_map/all_to_all | solution.py:83
  244.9 55.7 %all-to-all-start.1 = ((bf16[8,32,8192]{2,1,0:T(8,128)(2,1)}), bf16[8,32,8192]{2,1,0:T(8,128)(2,1)}, u32[]{:S(2)}, u32[]{:S(2)}) async-start(bf16[8,32,8192]{2,1,0:T(8,128)(2,1)} %copy.84), calls=%async_computation.1 | async-start | bytes 8388608 | tf_op jit(solution)/shard_map/all_to_all | solution.py:75
  300.6 54.3 %all-to-all-start.5 = ((bf16[8,32,8192]{2,1,0:T(8,128)(2,1)}), bf16[8,32,8192]{2,1,0:T(8,128)(2,1)}, u32[]{:S(2)}, u32[]{:S(2)}) async-start(bf16[8,32,8192]{2,1,0:T(8,128)(2,1)} %copy.90), calls=%async_computation.5 | async-start | bytes 8388608 | tf_op jit(solution)/shard_map/all_to_all | solution.py:82
  314.9 6.3 copy-start.2
  314.9 6.3 copy-start.4
  369.9 0.9 copy-start.12
  389.4 99.1 %all-to-all-start.2 = ((bf16[8,32,8192]{2,0,1:T(8,128)(2,1)}), bf16[8,32,8192]{2,0,1:T(8,128)(2,1)}, u32[]{:S(2)}, u32[]{:S(2)}) async-start(bf16[8,32,8192]{2,0,1:T(8,128)(2,1)} %copy.85), calls=%async_computation.2 | async-start | bytes 8388608 | tf_op jit(solution)/shard_map/all_to_all | solution.py:95
  394.5 3.7 copy-start.5
  394.5 3.7 copy-start.7
  488.6 104.3 %all-to-all-start.6 = ((bf16[8,32,8192]{2,0,1:T(8,128)(2,1)}), bf16[8,32,8192]{2,0,1:T(8,128)(2,1)}, u32[]{:S(2)}, u32[]{:S(2)}) async-start(bf16[8,32,8192]{2,0,1:T(8,128)(2,1)} %copy.91), calls=%async_computation.6 | async-start | bytes 8388608 | tf_op jit(solution)/shard_map/all_to_all | solution.py:108
  592.9 53.9 %all-to-all-start.3 = ((bf16[8,32,8192]{2,1,0:T(8,128)(2,1)}), bf16[8,32,8192]{2,1,0:T(8,128)(2,1)}, u32[]{:S(2)}, u32[]{:S(2)}) async-start(bf16[8,32,8192]{2,1,0:T(8,128)(2,1)} %copy.86), calls=%async_computation.3 | async-start | bytes 8388608 | tf_op jit(solution)/shard_map/all_to_all | solution.py:94
  605.4 48.5 %copy-start.13 = (bf16[1024,384]{1,0:T(8,128)(2,1)S(1)}, bf16[1024,384]{1,0:T(8,128)(2,1)}, u32[]{:S(2)}) copy-start(bf16[1024,384]{1,0:T(8,128)(2,1)} %copy-done.12) | copy-start | bytes 2359300
  646.8 58.7 %all-to-all-start.7 = ((bf16[8,32,8192]{2,1,0:T(8,128)(2,1)}), bf16[8,32,8192]{2,1,0:T(8,128)(2,1)}, u32[]{:S(2)}, u32[]{:S(2)}) async-start(bf16[8,32,8192]{2,1,0:T(8,128)(2,1)} %copy.92), calls=%async_computation.7 | async-start | bytes 8388608 | tf_op jit(solution)/shard_map/all_to_all | solution.py:107
  653.8 5.4 copy-start.3
  653.9 5.3 copy-start.8
  659.2 3.6 copy-start.6
  735.6 8.6 %copy-start.1 = (bf16[1,384,2048]{2,1,0:T(8,128)(2,1)S(1)}, bf16[1,384,2048]{2,1,0:T(8,128)(2,1)}, u32[]{:S(2)}) copy-start(bf16[1,384,2048]{2,1,0:T(8,128)(2,1)} %param.12) | copy-start | bytes 4718596
where the time goes:
time: 756 us; the launch traced here: 745 us
  waiting for transfers between devices  429 us (57%)
  local copies, waits for them, and re-layouts  173 us (23%)
  starting transfers between devices  68.7 us (9%)
  matrix products  41.6 us (6%)
  other arithmetic  30.3 us (4%)
    all_to_all x1, waiting for transfers between devices, local(): lax.all_to_all(pgrad.reshape(n_group, n_data, most * width), 'dp', split_...  90.9 us
    all_to_all x1, waiting for transfers between devices, local(): lax.all_to_all(qsend, 'dp', split_axis=1, concat_axis=1, tiled=True)  88 us
    all_to_all x1, waiting for transfers between devices, local(): lax.all_to_all(outv.reshape(n_group, n_data, most * width), 'dp', split_a...  71.7 us
    all_to_all x1, waiting for transfers between devices, local(): lax.all_to_all(xsend, 'dp', split_axis=1, concat_axis=1, tiled=True)  65.7 us
    all_to_all x1, waiting for transfers between devices, local(): lax.all_to_all(lax.all_to_all(xsend, 'dp', split_axis=1, concat_axis=1, t...  41.4 us
    all_to_all x1, waiting for transfers between devices, local(): lax.all_to_all(lax.all_to_all(outv.reshape(n_group, n_data, most * width)...  41.4 us
    all_to_all x1, waiting for transfers between devices, local(): lax.all_to_all(lax.all_to_all(qsend, 'dp', split_axis=1, concat_axis=1, t...  30.2 us
    all_to_all x1, starting transfers between devices, local(): lax.all_to_all(qsend, 'dp', split_axis=1, concat_axis=1, tiled=True)  18.5 us
  transfers between devices with their start and end apart: 8, of which 7 were waited for; matrix products, arithmetic and copies ran while one was open for 20% of the time, Pallas kernels for 0%

commit v1 on v0

--- a/solution.py
+++ b/solution.py
@@ -2,6 +2,22 @@
 import jax.numpy as jnp
 from jax import lax
 from jax.sharding import PartitionSpec as P
+
+
+def pairwise_exchange(x, axis, split, join):
+    ways, here = (lax.axis_size(axis), lax.axis_index(axis))
+    width = x.shape[split] // ways
+    shape = list(x.shape)
+    shape[split] = width
+    height = shape[join]
+    shape[join] = height * ways
+    full = jnp.zeros(shape, x.dtype)
+    for mask in range(ways):
+        part = lax.dynamic_slice_in_dim(x, (here ^ mask) * width, width, axis=split)
+        if mask:
+            part = lax.ppermute(part, axis, [(d, d ^ mask) for d in range(ways)])
+        full = lax.dynamic_update_slice_in_dim(full, part, (here ^ mask) * height, axis=join)
+    return full
 
 
 def expert_work(xrows, qrows, w_gate, w_up, w_down):
@@ -72,12 +88,8 @@
     xsend = tok_pad[row_token].reshape(n_group, n_data, most * width)
     qsend = q_pad[row_pair].reshape(n_group, n_data, most * width)
     xrecv, qrecv = (
-        lax.all_to_all(
-            lax.all_to_all(xsend, "dp", split_axis=1, concat_axis=1, tiled=True),
-            "expert",
-            split_axis=0,
-            concat_axis=0,
-            tiled=True,
+        pairwise_exchange(
+            lax.all_to_all(xsend, "dp", split_axis=1, concat_axis=1, tiled=True), "expert", 0, 0
         ),
         lax.all_to_all(
             lax.all_to_all(qsend, "dp", split_axis=1, concat_axis=1, tiled=True),

time: 756 us -> 739 us (0.978)
  waiting for transfers between devices: 429 us -> 375 us
  local copies, waits for them, and re-layouts: 173 us -> 215 us
    ppermute x0 -> x7, waiting for transfers between devices: none -> 53.6 us  [pairwise_exchange(): part = lax.ppermute(part, axis, [(d, d ^ mask) for d in range(ways)])]
    all_to_all x1 -> x0, waiting for transfers between devices: 41.4 us -> none  [local(): lax.all_to_all(lax.all_to_all(xsend, 'dp', split_axis=1, concat_axis=1, t...]
    all_to_all x1, waiting for transfers between devices: 41.4 us -> 0.01 us  [local(): lax.all_to_all(lax.all_to_all(outv.reshape(n_group, n_data, most * width)...]
    all_to_all x1, waiting for transfers between devices: 0.01 us -> 41.3 us  [local(): lax.all_to_all(lax.all_to_all(pgrad.reshape(n_group, n_data, most * width...]
    all_to_all x1, waiting for transfers between devices: 88 us -> 47.8 us  [local(): lax.all_to_all(qsend, 'dp', split_axis=1, concat_axis=1, tiled=True)]
    dynamic_slice x0 -> x8, local copies, waits for them, and re-layouts: none -> 32.2 us  [pairwise_exchange(): part = lax.dynamic_slice_in_dim(x, (here ^ mask) * width, width, axis=split)]
    all_to_all x1, waiting for transfers between devices: 30.2 us -> 0.01 us  [local(): lax.all_to_all(lax.all_to_all(qsend, 'dp', split_axis=1, concat_axis=1, t...]
    all_to_all x1, waiting for transfers between devices: 71.7 us -> 90.9 us  [local(): lax.all_to_all(outv.reshape(n_group, n_data, most * width), 'dp', split_a...]
  transfers between devices with their start and end apart: 8 -> 14, of which waited for: 7 -> 7; matrix products, arithmetic and copies ran while one was open for 20% -> 25% of each run, Pallas kernels for 0% -> 0%
where the time goes in v1:
time: 739 us; the launch traced here: 728 us
  waiting for transfers between devices  375 us (51%)
  local copies, waits for them, and re-layouts  215 us (29%)
  starting transfers between devices  67.6 us (9%)
  matrix products  38.2 us (5%)
  other arithmetic  30.5 us (4%)
    all_to_all x1, waiting for transfers between devices, local(): lax.all_to_all(outv.reshape(n_group, n_data, most * width), 'dp', split_a...  90.9 us
    all_to_all x1, waiting for transfers between devices, local(): lax.all_to_all(pgrad.reshape(n_group, n_data, most * width), 'dp', split_...  75.7 us
    all_to_all x1, waiting for transfers between devices, local(): lax.all_to_all(xsend, 'dp', split_axis=1, concat_axis=1, tiled=True)  65.6 us
    ppermute x7, waiting for transfers between devices, pairwise_exchange(): part = lax.ppermute(part, axis, [(d, d ^ mask) for d in range(ways)])  53.6 us
    all_to_all x1, waiting for transfers between devices, local(): lax.all_to_all(qsend, 'dp', split_axis=1, concat_axis=1, tiled=True)  47.8 us
    all_to_all x1, waiting for transfers between devices, local(): lax.all_to_all(lax.all_to_all(pgrad.reshape(n_group, n_data, most * width...  41.3 us
    dynamic_slice x8, local copies, waits for them, and re-layouts, pairwise_exchange(): part = lax.dynamic_slice_in_dim(x, (here ^ mask) * width, width, axis=split)  32.2 us
    ppermute x7, starting transfers between devices, pairwise_exchange(): part = lax.ppermute(part, axis, [(d, d ^ mask) for d in range(ways)])  19.1 us
  transfers between devices with their start and end apart: 14, of which 7 were waited for; matrix products, arithmetic and copies ran while one was open for 25% of the time, Pallas kernels for 0%

profile of v1, /device:TPU:11, one launch (start us, length us, event | category | flops | bytes accessed | tf_op | source)
XLA Modules:
  0.0 727.7 jit_solution(15128960298292120349)
XLA Ops:
  2.9 2.4 scatter_custom_fusion
  6.8 6.1 gather_fusion
  12.9 7.9 %reshape.463 = bf16[8,32,8192]{2,1,0:T(8,128)(2,1)} reshape(bf16[1024,2048]{1,0:T(8,128)(2,1)} %gather_fusion) | data formatting | bytes 8388608 | tf_op jit(solution)/shard_map/reshape | solution.py:88
  20.8 6.5 copy.104
  27.2 11.3 %all-to-all-start = ((bf16[8,32,8192]{2,0,1:T(8,128)(2,1)}), bf16[8,32,8192]{2,0,1:T(8,128)(2,1)}, u32[]{:S(2)}, u32[]{:S(2)}) async-start(bf16[8,32,8192]{2,0,1:T(8,128)(2,1)} %copy.104), calls=%async_computation | async-start | bytes 8388608 | tf_op jit(solution)/shard_map/all_to_all | solution.py:92
  38.9 2.4 mul.120
  41.3 3.7 mul.121
  45.0 1.8 multiply_convert_fusion
  46.9 6.0 gather_fusion.2
  52.9 8.0 %reshape.467 = bf16[8,32,8192]{2,1,0:T(8,128)(2,1)} reshape(bf16[1024,2048]{1,0:T(8,128)(2,1)} %gather_fusion.2) | data formatting | bytes 8388608 | tf_op jit(solution)/shard_map/reshape | solution.py:89
  60.9 6.5 copy.117
  67.3 65.6 %all-to-all-done = bf16[8,32,8192]{2,0,1:T(8,128)(2,1)} async-done(((bf16[8,32,8192]{2,0,1:T(8,128)(2,1)}), bf16[8,32,8192]{2,0,1:T(8,128)(2,1)}, u32[]{:S(2)}, u32[]{:S(2)}) %all-to-all-start) | async-done | bytes 4194336 | tf_op jit(solution)/shard_map/all_to_all | solution.py:92
  133.0 7.5 %all-to-all-start.3 = ((bf16[8,32,8192]{2,0,1:T(8,128)(2,1)}), bf16[8,32,8192]{2,0,1:T(8,128)(2,1)}, u32[]{:S(2)}, u32[]{:S(2)}) async-start(bf16[8,32,8192]{2,0,1:T(8,128)(2,1)} %copy.117), calls=%async_computation.3 | async-start | bytes 8388608 | tf_op jit(solution)/shard_map/all_to_all | solution.py:95
  140.5 22.2 %constant_dynamic-slice_fusion = (bf16[1,32,8192]{2,0,1:T(2,128)(2,1)S(1)}, bf16[1,32,8192]{2,0,1:T(2,128)(2,1)S(1)}, bf16[1,32,8192]{2,0,1:T(2,128)(2,1)S(1)}, ...) fusion(bf16[8,32,8192]{2,0,1:T(8,128)(2,1)} %all-to-all-done, ...), kind=kLoop, calls=%fused_computation.76 | loop fusion | bytes 8388640 | tf_op jit(solution)/shard_map/dynamic_slice | solution.py:16
  162.7 2.6 copy.106
  172.1 1.8 collective-permute-start.3
  175.3 12.6 %collective-permute-start.4 = (bf16[1,32,8192]{2,1,0:T(8,128)(2,1)}, bf16[1,32,8192]{2,1,0:T(8,128)(2,1)}, u32[]{:S(2)}, u32[]{:S(2)}) collective-permute-start(bf16[1,32,8192]{2,1,0:T(8,128)(2,1)} %copy.110), channel_id=1, source_target_pairs={{0,5},{1,4},{2,7},{3,6},{4,1},{5,0},{6,3},{7,2},{8,13},{9,12},{10,... | collective-permute-start | bytes 1572872 | tf_op jit(solution)/shard_map/ppermute | solution.py:18
  189.9 47.8 %all-to-all-done.3 = bf16[8,32,8192]{2,0,1:T(8,128)(2,1)} async-done(((bf16[8,32,8192]{2,0,1:T(8,128)(2,1)}), bf16[8,32,8192]{2,0,1:T(8,128)(2,1)}, u32[]{:S(2)}, u32[]{:S(2)}) %all-to-all-start.3) | async-done | bytes 4194336 | tf_op jit(solution)/shard_map/all_to_all | solution.py:95
  237.7 6.5 copy.118
  244.2 5.1 all-to-all-start.4
  249.3 2.4 broadcast_in_dim.14
  254.3 1.9 constant_dynamic-update-slice_fusion.6
  256.9 1.9 constant_dynamic-update-slice_fusion.5
  258.8 1.9 constant_dynamic-update-slice_fusion.4
  260.7 1.9 constant_dynamic-update-slice_fusion.3
  262.7 1.9 constant_dynamic-update-slice_fusion.2
  264.5 43.0 %collective-permute-done.5 = bf16[1,32,8192]{2,1,0:T(8,128)(2,1)S(1)} collective-permute-done((bf16[1,32,8192]{2,1,0:T(8,128)(2,1)S(1)}, bf16[1,32,8192]{2,1,0:T(8,128)(2,1)S(1)}, u32[]{:S(2)}, u32[]{:S(2)}) %collective-permute-start.5) | collective-permute-done | bytes 524320 | tf_op jit(solution)/shard_map/ppermute | solution.py:18
  308.5 10.6 %collective-permute-done.6 = bf16[1,32,8192]{2,1,0:T(8,128)(2,1)S(1)} collective-permute-done((bf16[1,32,8192]{2,1,0:T(8,128)(2,1)S(1)}, bf16[1,32,8192]{2,1,0:T(8,128)(2,1)S(1)}, u32[]{:S(2)}, u32[]{:S(2)}) %collective-permute-start.6) | collective-permute-done | bytes 524320 | tf_op jit(solution)/shard_map/ppermute | solution.py:18
  319.9 8.1 %reshape.464 = bf16[1024,2048]{1,0:T(8,128)(2,1)} reshape(bf16[8,32,8192]{2,1,0:T(8,128)(2,1)} %constant_dynamic-update-slice_fusion) | data formatting | bytes 8388608 | tf_op jit(solution)/shard_map/reshape | solution.py:103
  327.9 5.6 fusion.7
  333.6 8.0 %reshape.468 = bf16[1024,2048]{1,0:T(8,128)(2,1)} reshape(bf16[8,32,8192]{2,1,0:T(8,128)(2,1)} %all-to-all-done.4) | data formatting | bytes 8388608 | tf_op jit(solution)/shard_map/reshape | solution.py:103
  341.5 5.2 fusion.3
  346.7 3.9 multiply_convert_fusion.1
  350.7 2.4 fusion.9
  353.1 4.3 add_convert_fusion
  357.4 8.3 %reshape.469 = bf16[8,32,8192]{2,1,0:T(8,128)(2,1)} reshape(bf16[1024,2048]{1,0:T(8,128)(2,1)} %add_convert_fusion) | data formatting | bytes 8388608 | tf_op jit(solution)/shard_map/reshape | solution.py:121
  365.7 6.4 copy.119
  372.1 4.8 all-to-all-start.5
  376.9 4.3 convolution_convert_fusion
  381.2 7.9 %reshape.465 = bf16[8,32,8192]{2,1,0:T(8,128)(2,1)} reshape(bf16[1024,2048]{1,0:T(8,128)(2,1)} %convolution_convert_fusion) | data formatting | bytes 8388608 | tf_op jit(solution)/shard_map/reshape | solution.py:108
  389.1 6.4 copy.113
  395.6 75.7 %all-to-all-done.5 = bf16[8,32,8192]{2,0,1:T(8,128)(2,1)} async-done(((bf16[8,32,8192]{2,0,1:T(8,128)(2,1)}), bf16[8,32,8192]{2,0,1:T(8,128)(2,1)}, u32[]{:S(2)}, u32[]{:S(2)}) %all-to-all-start.5) | async-done | bytes 4194336 | tf_op jit(solution)/shard_map/all_to_all | solution.py:120
  471.2 7.0 all-to-all-start.1
  478.3 6.5 copy.120
  484.7 90.9 %all-to-all-done.1 = bf16[8,32,8192]{2,0,1:T(8,128)(2,1)} async-done(((bf16[8,32,8192]{2,0,1:T(8,128)(2,1)}), bf16[8,32,8192]{2,0,1:T(8,128)(2,1)}, u32[]{:S(2)}, u32[]{:S(2)}) %all-to-all-start.1) | async-done | bytes 4194336 | tf_op jit(solution)/shard_map/all_to_all | solution.py:107
  575.7 6.4 all-to-all-start.6
  582.1 6.5 copy.114
  588.5 41.3 %all-to-all-done.6 = bf16[8,32,8192]{2,1,0:T(8,128)(2,1)} async-done(((bf16[8,32,8192]{2,1,0:T(8,128)(2,1)}), bf16[8,32,8192]{2,1,0:T(8,128)(2,1)}, u32[]{:S(2)}, u32[]{:S(2)}) %all-to-all-start.6) | async-done | bytes 4194336 | tf_op jit(solution)/shard_map/all_to_all | solution.py:119
  629.9 6.4 all-to-all-start.2
  636.8 5.3 fusion.2
  642.1 3.6 fusion.1
  645.7 3.6 fusion
  649.3 8.0 %reshape.470 = bf16[1024,2048]{1,0:T(8,128)(2,1)} reshape(bf16[8,32,8192]{2,1,0:T(8,128)(2,1)} %all-to-all-done.6) | data formatting | bytes 8388608 | tf_op jit(solution)/shard_map/reshape | solution.py:135
  657.3 8.0 %gather_fusion.3 = bf16[512,2048]{1,0:T(8,128)(2,1)} fusion(bf16[1024,2048]{1,0:T(8,128)(2,1)} %reshape.470, s32[1024]{0:T(1024)S(1)} %pad_clamp_fusion), kind=kCustom, calls=%fused_computation.3 | custom fusion | bytes 4196352 | tf_op jit(solution)/shard_map/gather | solution.py:135
  665.2 5.7 reshape.515
  670.9 8.6 %reduce_sum.51 = f32[256,2048]{1,0:T(8,128)} reduce(f32[256,2,2048]{2,1,0:T(2,128)} %reshape.515, f32[]{:T(128)} %constant.100.clone.1), dimensions={1}, to_apply=%region_6.7 | reduce | flops 524288 | bytes 6291460 | tf_op jit(solution)/shard_map/reduce_sum | solution.py:135
  679.5 3.5 reshape.471
  683.0 5.0 reduce_sum.52
  688.0 7.9 %reshape.466 = bf16[1024,2048]{1,0:T(8,128)(2,1)} reshape(bf16[8,32,8192]{2,1,0:T(8,128)(2,1)} %all-to-all-done.2) | data formatting | bytes 8388608 | tf_op jit(solution)/shard_map/reshape | solution.py:134
  695.9 8.0 %gather_fusion.1 = bf16[512,2048]{1,0:T(8,128)(2,1)} fusion(bf16[1024,2048]{1,0:T(8,128)(2,1)} %reshape.466, s32[1024]{0:T(1024)S(1)} %pad_clamp_fusion), kind=kCustom, calls=%fused_computation.1 | custom fusion | bytes 4196352 | tf_op jit(solution)/shard_map/gather | solution.py:134
  703.8 5.7 reshape.514
  709.6 8.7 %reduce_sum.48 = f32[256,2048]{1,0:T(8,128)} reduce(f32[256,2,2048]{2,1,0:T(2,128)} %reshape.514, f32[]{:T(128)} %constant.100.clone.1), dimensions={1}, to_apply=%region_4.5 | reduce | flops 524288 | bytes 6291460 | tf_op jit(solution)/shard_map/reduce_sum | solution.py:134
  718.2 3.5 reduce_sum.49
  721.7 5.6 multiply_reduce_fusion
  (83 shorter events, 19.7 us)
Async XLA Ops:
  0.6 346.1 %copy-start = (bf16[1,2048,384]{2,1,0:T(8,128)(2,1)S(1)}, bf16[1,2048,384]{2,1,0:T(8,128)(2,1)}, u32[]{:S(2)}) copy-start(bf16[1,2048,384]{2,1,0:T(8,128)(2,1)} %param.10) | copy-start | bytes 4718596
  27.2 11.3 %copy-start.11 = (s32[128,2]{0,1:T(2,128)S(1)}, s32[128,2]{0,1:T(2,128)}, u32[]{:S(2)}) copy-start(s32[128,2]{0,1:T(2,128)} %param.9) | copy-start | bytes 3076
  27.2 11.6 %copy-start.9 = (bf16[128,2048]{1,0:T(8,128)(2,1)S(1)}, bf16[128,2048]{1,0:T(8,128)(2,1)}, u32[]{:S(2)}) copy-start(bf16[128,2048]{1,0:T(8,128)(2,1)} %param.13) | copy-start | bytes 1572868
  27.2 105.7 %all-to-all-start = ((bf16[8,32,8192]{2,0,1:T(8,128)(2,1)}), bf16[8,32,8192]{2,0,1:T(8,128)(2,1)}, u32[]{:S(2)}, u32[]{:S(2)}) async-start(bf16[8,32,8192]{2,0,1:T(8,128)(2,1)} %copy.104), calls=%async_computation | async-start | bytes 8388608 | tf_op jit(solution)/shard_map/all_to_all | solution.py:92
  133.0 104.7 %all-to-all-start.3 = ((bf16[8,32,8192]{2,0,1:T(8,128)(2,1)}), bf16[8,32,8192]{2,0,1:T(8,128)(2,1)}, u32[]{:S(2)}, u32[]{:S(2)}) async-start(bf16[8,32,8192]{2,0,1:T(8,128)(2,1)} %copy.117), calls=%async_computation.3 | async-start | bytes 8388608 | tf_op jit(solution)/shard_map/all_to_all | solution.py:95
  165.3 87.7 %collective-permute-start = (bf16[1,32,8192]{2,1,0:T(8,128)(2,1)}, bf16[1,32,8192]{2,1,0:T(8,128)(2,1)}, u32[]{:S(2)}, u32[]{:S(2)}) collective-permute-start(bf16[1,32,8192]{2,1,0:T(8,128)(2,1)} %copy.106), channel_id=1, source_target_pairs={{0,1},{1,0},{2,3},{3,2},{4,5},{5,4},{6,7},{7,6},{8,9},{9,8},{10,11... | collective-permute-start | bytes 1572872 | tf_op jit(solution)/shard_map/ppermute | solution.py:18
  167.7 88.4 %collective-permute-start.1 = (bf16[1,32,8192]{2,1,0:T(8,128)(2,1)}, bf16[1,32,8192]{2,1,0:T(8,128)(2,1)}, u32[]{:S(2)}, u32[]{:S(2)}) collective-permute-start(bf16[1,32,8192]{2,1,0:T(8,128)(2,1)} %copy.107), channel_id=1, source_target_pairs={{0,2},{1,3},{2,0},{3,1},{4,6},{5,7},{6,4},{7,5},{8,10},{9,11},{10,... | collective-permute-start | bytes 1572872 | tf_op jit(solution)/shard_map/ppermute | solution.py:18
  169.3 89.5 %collective-permute-start.2 = (bf16[1,32,8192]{2,1,0:T(8,128)(2,1)}, bf16[1,32,8192]{2,1,0:T(8,128)(2,1)}, u32[]{:S(2)}, u32[]{:S(2)}) collective-permute-start(bf16[1,32,8192]{2,1,0:T(8,128)(2,1)} %copy.108), channel_id=1, source_target_pairs={{0,3},{1,2},{2,1},{3,0},{4,7},{5,6},{6,5},{7,4},{8,11},{9,10},{10,... | collective-permute-start | bytes 1572872 | tf_op jit(solution)/shard_map/ppermute | solution.py:18
  172.1 88.6 %collective-permute-start.3 = (bf16[1,32,8192]{2,1,0:T(8,128)(2,1)}, bf16[1,32,8192]{2,1,0:T(8,128)(2,1)}, u32[]{:S(2)}, u32[]{:S(2)}) collective-permute-start(bf16[1,32,8192]{2,1,0:T(8,128)(2,1)} %copy.109), channel_id=1, source_target_pairs={{0,4},{1,5},{2,6},{3,7},{4,0},{5,1},{6,2},{7,3},{8,12},{9,13},{10,... | collective-permute-start | bytes 1572872 | tf_op jit(solution)/shard_map/ppermute | solution.py:18
  175.3 87.3 %collective-permute-start.4 = (bf16[1,32,8192]{2,1,0:T(8,128)(2,1)}, bf16[1,32,8192]{2,1,0:T(8,128)(2,1)}, u32[]{:S(2)}, u32[]{:S(2)}) collective-permute-start(bf16[1,32,8192]{2,1,0:T(8,128)(2,1)} %copy.110), channel_id=1, source_target_pairs={{0,5},{1,4},{2,7},{3,6},{4,1},{5,0},{6,3},{7,2},{8,13},{9,12},{10,... | collective-permute-start | bytes 1572872 | tf_op jit(solution)/shard_map/ppermute | solution.py:18
  244.2 89.4 %all-to-all-start.4 = ((bf16[8,32,8192]{2,1,0:T(8,128)(2,1)}), bf16[8,32,8192]{2,1,0:T(8,128)(2,1)}, u32[]{:S(2)}, u32[]{:S(2)}) async-start(bf16[8,32,8192]{2,1,0:T(8,128)(2,1)} %copy.118), calls=%async_computation.4 | async-start | bytes 8388608 | tf_op jit(solution)/shard_map/all_to_all | solution.py:94
  249.3 3.8 copy-start.10
  253.0 54.6 %collective-permute-start.5 = (bf16[1,32,8192]{2,1,0:T(8,128)(2,1)S(1)}, bf16[1,32,8192]{2,1,0:T(8,128)(2,1)S(1)}, u32[]{:S(2)}, u32[]{:S(2)}) collective-permute-start(bf16[1,32,8192]{2,1,0:T(8,128)(2,1)S(1)} %copy-done.10), channel_id=1, source_target_pairs={{0,6},{1,7},{2,4},{3,5},{4,2},{5,3},{6,0},{7,1},{8,14},{9,15},{10,... | collective-permute-start | bytes 1572872 | tf_op jit(solution)/shard_map/ppermute | solution.py:18
  256.1 62.9 %collective-permute-start.6 = (bf16[1,32,8192]{2,1,0:T(8,128)(2,1)S(1)}, bf16[1,32,8192]{2,1,0:T(8,128)(2,1)S(1)}, u32[]{:S(2)}, u32[]{:S(2)}) collective-permute-start(bf16[1,32,8192]{2,1,0:T(8,128)(2,1)S(1)} %copy.112), channel_id=1, source_target_pairs={{0,7},{1,6},{2,5},{3,4},{4,3},{5,2},{6,1},{7,0},{8,15},{9,14},{10,... | collective-permute-start | bytes 1572872 | tf_op jit(solution)/shard_map/ppermute | solution.py:18
  319.8 8.1 %copy-start.4 = (bf16[1,2048,384]{2,1,0:T(8,128)(2,1)S(1)}, bf16[1,2048,384]{2,1,0:T(8,128)(2,1)}, u32[]{:S(2)}) copy-start(bf16[1,2048,384]{2,1,0:T(8,128)(2,1)} %param.11) | copy-start | bytes 4718596
  341.5 5.2 copy-start.2
  341.5 5.2 copy-start.14
  350.7 2.4 copy-start.5
  350.7 2.4 copy-start.7
  372.1 4.8 copy-start.12
  372.1 4.8 copy-start.13
  372.1 99.2 %all-to-all-start.5 = ((bf16[8,32,8192]{2,0,1:T(8,128)(2,1)}), bf16[8,32,8192]{2,0,1:T(8,128)(2,1)}, u32[]{:S(2)}, u32[]{:S(2)}) async-start(bf16[8,32,8192]{2,0,1:T(8,128)(2,1)} %copy.119), calls=%async_computation.5 | async-start | bytes 8388608 | tf_op jit(solution)/shard_map/all_to_all | solution.py:120
  471.2 104.4 %all-to-all-start.1 = ((bf16[8,32,8192]{2,0,1:T(8,128)(2,1)}), bf16[8,32,8192]{2,0,1:T(8,128)(2,1)}, u32[]{:S(2)}, u32[]{:S(2)}) async-start(bf16[8,32,8192]{2,0,1:T(8,128)(2,1)} %copy.113), calls=%async_computation.1 | async-start | bytes 8388608 | tf_op jit(solution)/shard_map/all_to_all | solution.py:107
  575.7 54.2 %all-to-all-start.6 = ((bf16[8,32,8192]{2,1,0:T(8,128)(2,1)}), bf16[8,32,8192]{2,1,0:T(8,128)(2,1)}, u32[]{:S(2)}, u32[]{:S(2)}) async-start(bf16[8,32,8192]{2,1,0:T(8,128)(2,1)} %copy.120), calls=%async_computation.6 | async-start | bytes 8388608 | tf_op jit(solution)/shard_map/all_to_all | solution.py:119
  629.9 58.1 %all-to-all-start.2 = ((bf16[8,32,8192]{2,1,0:T(8,128)(2,1)}), bf16[8,32,8192]{2,1,0:T(8,128)(2,1)}, u32[]{:S(2)}, u32[]{:S(2)}) async-start(bf16[8,32,8192]{2,1,0:T(8,128)(2,1)} %copy.114), calls=%async_computation.2 | async-start | bytes 8388608 | tf_op jit(solution)/shard_map/all_to_all | solution.py:106
  636.8 5.3 copy-start.3
  636.8 5.3 copy-start.8
  642.1 3.6 copy-start.6
  709.6 17.7 %copy-start.1 = (bf16[1,2048,384]{2,1,0:T(8,128)(2,1)S(1)}, bf16[1,2048,384]{2,1,0:T(8,128)(2,1)}, u32[]{:S(2)}) copy-start(bf16[1,2048,384]{2,1,0:T(8,128)(2,1)} %param.10) | copy-start | bytes 4718596
